TPU v7x, 256 devices: a whole 4x4x8 slice. The times are simulated.
256 devices in a mesh: dp: 64 (over x, z, core), tensor: 4 (over y).
Axes of the slice: x: 4, y: 4, z: 8, core: 2. Of those that a mesh axis runs over, the one named last changes fastest.
Arguments:
- tokens: bfloat16 [512, 16384], P('dp', 'tensor'), may hold values from -6 to 6
- clip_act: float32 [16384], P('tensor'), may hold values from 0.5 to 4
- weight: bfloat16 [16384, 49152], P('tensor', 'dp'), may hold values from -0.046875 to 0.046875
- clip_weight: float32 [49152], P('dp'), may hold values from 0.003 to 0.03
- cotangent: bfloat16 [512, 49152], P('tensor', 'dp'), may hold values from -16 to 16
Outputs:
- projected: bfloat16 [512, 49152], P('tensor', 'dp')
- token_grad: bfloat16 [512, 16384], P('dp', 'tensor')
- weight_grad: bfloat16 [16384, 49152], P('tensor', 'dp')
- clip_act_grad: float32 [16384], P('tensor')
- clip_weight_grad: float32 [49152], P('dp')
All inputs are finite; a program needn't handle non-finite values.
Results may differ from a plain program's by a relative error of at most 0.009.
Values may be sent and summed in bfloat16 or wider, within the bound.
No kernel may reach another device: no remote copies, remote signals or barrier semaphores. Data moves between devices by JAX's collectives and lax.ppermute only.
A program may use at most 128 MiB of HBM per device.

v0:
```python
import math
import jax
import jax.numpy as jnp
from jax import lax
from jax.sharding import PartitionSpec as P


def swapped(block, axis, bit):
    count = lax.axis_size(axis)
    route = []
    for low in range(count):
        high = low | 1 << bit
        if high != low and high < count:
            route += [(low, high), (high, low)]
    return lax.ppermute(block, axis, route)


def sylvester(order):
    index = lax.iota(jnp.int32, order)
    joined = jnp.bitwise_and(index[:, None], index[None, :])
    parity = jnp.zeros((order, order), jnp.int32)
    for bit_number in range(max(order.bit_length() - 1, 0)):
        parity = parity + jnp.bitwise_and(jnp.right_shift(joined, bit_number), 1)
    return (1 - 2 * jnp.bitwise_and(parity, 1)).astype(jnp.float32)


def local_rotate(values, norm_factor):
    row_total, width = values.shape
    levels = width.bit_length() - 1
    outer = 2 ** (levels // 2)
    inner = width // outer
    blocks = values.reshape(row_total, outer, inner)
    blocks = jnp.einsum("rab,ac->rcb", blocks, sylvester(outer), precision=lax.Precision.HIGHEST)
    blocks = jnp.einsum("rcb,bd->rcd", blocks, sylvester(inner), precision=lax.Precision.HIGHEST)
    return blocks.reshape(row_total, width) * norm_factor


def rotate(values):
    group_size = lax.axis_size("tensor")
    norm_factor = 1.0 / math.sqrt(values.shape[1] * group_size)
    mixed = local_rotate(values, norm_factor)
    position = lax.axis_index("tensor")
    for bit_number in range(group_size.bit_length() - 1):
        partner = swapped(mixed, "tensor", bit_number)
        upper = jnp.bitwise_and(jnp.right_shift(position, bit_number), 1) == 1
        mixed = jnp.where(upper, partner - mixed, mixed + partner)
    return mixed


def body(tokens, clip_act, weight, clip_weight, cotangent):
    rotated = rotate(tokens.astype(jnp.float32))
    ratio_act = rotated / clip_act
    tanh_act = jnp.tanh(ratio_act)
    quant_act = (clip_act * tanh_act).astype(jnp.bfloat16)
    slope_act = 1.0 - tanh_act * tanh_act
    edge_act = tanh_act - ratio_act * slope_act
    rows, width = quant_act.shape
    chips = lax.axis_size("dx") * lax.axis_size("dz")
    cores = lax.axis_size("dc")
    core = lax.axis_index("dc")
    ratio_weight = weight.astype(jnp.float32) / clip_weight
    tanh_weight = jnp.tanh(ratio_weight)
    quant_weight = (clip_weight * tanh_weight).astype(jnp.bfloat16)
    all_cot = lax.all_gather(cotangent, "tensor", axis=0, tiled=True)
    partial = lax.dot_general(
        all_cot, quant_weight, (((1,), (1,)), ((), ())), preferred_element_type=jnp.float32
    ).reshape(chips, cores, rows, width)
    quant_act, partial = lax.optimization_barrier((quant_act, partial))
    half_act = lax.all_gather(quant_act, CHIPS, axis=0, tiled=True)
    pair = [(0, 1), (1, 0)]
    partner_act = lax.ppermute(half_act, "dc", pair)
    both_act = jnp.where(
        core == 0, jnp.stack([half_act, partner_act]), jnp.stack([partner_act, half_act])
    )
    all_act = both_act.reshape(cores, chips, rows, width).transpose(1, 0, 2, 3).reshape(-1, width)
    block = all_act
    projected = lax.psum_scatter(
        jnp.dot(block, quant_weight, preferred_element_type=jnp.float32),
        "tensor",
        scatter_dimension=0,
        tiled=True,
    ).astype(jnp.bfloat16)
    weight_prod = lax.dot_general(
        all_act, all_cot, (((0,), (0,)), ((), ())), preferred_element_type=jnp.float32
    )
    slope_weight = 1.0 - tanh_weight * tanh_weight
    weight_grad = (weight_prod * slope_weight).astype(jnp.bfloat16)
    weight_terms = jnp.sum(weight_prod * (tanh_weight - ratio_weight * slope_weight), axis=0)
    clip_weight_grad = lax.psum(weight_terms, "tensor")
    mine = lax.dynamic_index_in_dim(partial, core, axis=1, keepdims=False)
    other = lax.dynamic_index_in_dim(partial, cores - 1 - core, axis=1, keepdims=False)
    chip_sum = mine + lax.ppermute(other.astype(jnp.bfloat16), "dc", pair).astype(jnp.float32)
    pieces = lax.all_to_all(chip_sum.astype(jnp.bfloat16), CHIPS, 0, 0, tiled=True)
    act_prod = jnp.sum(pieces.astype(jnp.float32), axis=0)
    act_terms = jnp.sum(act_prod * edge_act, axis=0)
    groups = lax.axis_size("tensor")
    slots = jnp.zeros((groups,) + act_terms.shape, act_terms.dtype)
    slots = lax.dynamic_update_index_in_dim(slots, act_terms, lax.axis_index("tensor"), 0)
    slots = lax.psum(slots, DP + ("tensor",))
    clip_act_grad = lax.dynamic_index_in_dim(slots, lax.axis_index("tensor"), 0, keepdims=False)
    pre_rotation = act_prod * slope_act
    token_grad = rotate(pre_rotation).astype(jnp.bfloat16)
    return (projected, token_grad, weight_grad, clip_act_grad, clip_weight_grad)


DP = ("dx", "dz", "dc")
CHIPS = ("dx", "dz")


def solution(mesh):
    rows, cols = mesh.devices.shape
    cores = 2
    across = 4 if rows % (4 * cores) == 0 else 1
    grid = mesh.devices.reshape(across, rows // (across * cores), cores, cols)
    fine = jax.sharding.Mesh(grid, ("dx", "dz", "dc", "tensor"))
    in_specs = (P(DP, "tensor"), P("tensor"), P("tensor", DP), P(DP), P("tensor", DP))
    out_specs = (P("tensor", DP), P(DP, "tensor"), P("tensor", DP), P("tensor"), P(DP))
    return jax.shard_map(body, mesh=fine, in_specs=in_specs, out_specs=out_specs, check_vma=False)
```

profile of v0, /device:TPU:1, one launch (start us, length us, event | category | flops | bytes accessed | tf_op | source)
XLA Modules:
  0.0 391.6 jit_solution(14210989227953233177)
XLA Ops:
  8.0 0.0 all-gather.2.cloned.1.call-start
  8.0 1.0 reshape.40
  9.1 0.3 convolution_bitcast_fusion.1
  9.4 0.4 convolution_multiply_fusion.1
  9.8 0.1 mul.67
  9.9 0.0 copy-start.2
  9.9 2.2 collective-permute-start
  12.1 7.3 %multiply_convert_fusion.1 = bf16[4096,768]{1,0:T(8,128)(2,1)} fusion(f32[768]{0:T(1024)} %param.8, bf16[4096,768]{1,0:T(8,128)(2,1)} %param.7), kind=kLoop, calls=%fused_computation.3 | loop fusion | flops 12582912 | bytes 12585984 | tf_op jit(solution)/shard_map/convert_element_type | solution.py:63
  19.4 0.0 copy-done.2
  19.4 11.8 %all_gather.6 = bf16[512,768]{1,0:T(8,128)(2,1)S(1)} all-gather(bf16[128,768]{1,0:T(8,128)(2,1)S(1)} %copy-done.2), channel_id=1, replica_groups=mesh['dx'=4,'dz'=8,'dc'=2,'tensor'=4] {'tensor'}, dimensions={0}, use_global_device_ids=true | all-gather | bytes 983040 | tf_op jit(solution)/shard_map/all_gather | solution.py:64
  31.2 0.0 collective-permute-done
  31.2 0.0 copy-start.3
  31.2 1.3 collective-permute-start.1
  32.5 8.4 %fusion.35 = f32[4096,512]{0,1:T(8,128)} fusion(bf16[4096,768]{1,0:T(8,128)(2,1)} %multiply_convert_fusion.1, bf16[512,768]{1,0:T(8,128)(2,1)S(1)} %all_gather.6), kind=kOutput, calls=%fused_computation.57 | convolution fusion | flops 3221225472 | bytes 15466496 | tf_op jit(solution)/shard_map/dot_general | solution.py:65
  40.9 0.0 collective-permute-done.1
  40.9 0.0 copy-done.3
  40.9 0.7 multiply_convert_fusion.2
  41.6 2.5 fusion.1
  44.1 3.5 collective-permute-start.3
  47.6 0.0 all-gather.2.cloned.1.call-update
  47.6 3.9 collective-permute-done.3
  51.5 4.7 %fusion = bf16[32,8,4096]{2,1,0:T(8,128)(2,1)} fusion(bf16[32,8,4096]{2,1,0:T(8,128)(2,1)} %collective-permute-done.3, f32[32,2,8,4096]{3,2,1,0:T(8,128)} %bitcast.40, s32[]{:T(128)S(6)} %select_n.50), kind=kLoop, calls=%fused_computation.7 | loop fusion | flops 3145728 | bytes 8388612 | tf_op jit(solution)/shard_map/convert_element_type | solution.py:93
  56.3 11.0 %all-to-all-start = ((bf16[32,8,4096]{2,1,0:T(8,128)(2,1)}), bf16[32,8,4096]{2,1,0:T(8,128)(2,1)S(1)}, u32[]{:S(2)}, u32[]{:S(2)}) async-start(bf16[32,8,4096]{2,1,0:T(8,128)(2,1)} %fusion), calls=%async_computation.1 | async-start | bytes 4194304 | tf_op jit(solution)/shard_map/all_to_all | solution.py:93
  67.3 0.0 all-reduce.2.cloned.1.call-start
  67.4 66.5 %all-gather.2.cloned.1.call-done = bf16[256,4096]{1,0:T(8,128)(2,1)} async-done(((bf16[8,4096]{1,0:T(8,128)(2,1)}), bf16[256,4096]{1,0:T(8,128)(2,1)}) %all-gather.2.cloned.1.call-update) | async-done | bytes 2097168 | tf_op jit(solution)/shard_map/all_gather | solution.py:69
  133.8 2.7 collective-permute-start.2
  136.5 0.0 all-to-all-done
  136.5 0.3 convert_reduce_fusion
  136.8 0.1 multiply_reduce_fusion.1
  136.9 0.1 reshape.43
  137.0 0.4 convolution_bitcast_fusion
  137.4 0.4 convolution_multiply_fusion
  137.8 0.1 mul.74
  137.9 1.3 collective-permute-start.4
  139.2 0.2 dynamic_update_slice.4
  139.5 0.0 copy-start.1
  139.5 0.6 copy-done.1
  140.1 0.0 all-reduce.2.cloned.1.call-update
  140.2 0.2 reduce-scatter.2.cloned.1.call-start
  140.4 0.3 collective-permute-done.2
  140.7 4.1 %maximum_select_fusion = bf16[2,32,8,4096]{3,2,0,1:T(8,128)(2,1)S(1)} fusion(bf16[1,32,8,4096]{3,2,0,1:T(8,128)(2,1)} %bitcast.5, bf16[1,32,8,4096]{3,2,0,1:T(8,128)(2,1)} %bitcast.43, pred[]{:T(512)S(6)} %eq.11), kind=kLoop, calls=%fused_computation.5 | loop fusion | flops 6291456 | bytes 8388609 | tf_op jit(solution)/shard_map/jit(_where)/select_n | solution.py:72
  144.7 0.0 copy-start
  144.7 1.9 copy-done
  146.7 0.0 copy-start.4
  146.7 6.7 %fusion.36 = f32[512,768]{1,0:T(8,128)} fusion(bf16[512,4096]{1,0:T(8,128)(2,1)S(1)} %bitcast.41, bf16[4096,768]{1,0:T(8,128)(2,1)} %multiply_convert_fusion.1), kind=kOutput, calls=%fused_computation.58 | convolution fusion | flops 3221225472 | bytes 12058624 | tf_op jit(solution)/shard_map/dot_general | solution.py:78
  153.3 0.0 reduce-scatter.2.cloned.1.call-update
  153.4 0.0 copy-done.4
  153.4 12.5 %multiply_reduce_fusion = (f32[768]{0:T(1024)S(1)}, bf16[4096,768]{1,0:T(8,128)(2,1)}) fusion(f32[768]{0:T(1024)S(1)} %copy-done.4, bf16[4096,768]{1,0:T(8,128)(2,1)} %param.7, bf16[512,4096]{1,0:T(8,128)(2,1)} %bitcast.42, bf16[512,768]{1,0:T(8,128)(2,1)S(1)} %all_gather.6), kind=kOutput, calls=%fused_computation | convolution fusion | flops 3252681984 | bytes 17569792 | tf_op jit(solution)/shard_map/dot_general | solution.py:83
  165.8 10.0 %psum.15 = f32[768]{0:T(1024)} all-reduce(f32[768]{0:T(1024)S(1)} %get-tuple-element.11), channel_id=1, replica_groups=mesh['dx'=4,'dz'=8,'dc'=2,'tensor'=4] {'tensor'}, use_global_device_ids=true, to_apply=%region_5.6 | all-reduce | flops 768 | bytes 6144 | tf_op jit(solution)/shard_map/psum | solution.py:89
  175.8 0.0 collective-permute-done.4
  175.8 0.7 collective-permute-start.5
  176.5 203.9 %all-reduce.2.cloned.1.call-done = f32[4,4096]{1,0:T(4,128)} async-done(((f32[4,4096]{1,0:T(4,128)}), f32[4,4096]{1,0:T(4,128)}) %all-reduce.2.cloned.1.call-update) | async-done | bytes 65552 | tf_op jit(solution)/shard_map/psum | solution.py:99
  380.4 1.5 constant_dynamic-slice_fusion
  381.8 0.0 collective-permute-done.5
  381.8 0.6 select_convert_fusion
  382.5 0.0 reduce-scatter.2.cloned.1.call-done
  382.5 1.7 convert_element_type.50
  (3 shorter events, 0.0 us)
Async XLA Ops:
  8.0 125.8 %all-gather.2.cloned.1.call-start = ((), (), s32[]{:S(2)}) async-start(), calls=%async_computation.2 | async-start | bytes 2162688 | tf_op jit(solution)/shard_map/all_gather | solution.py:69
  9.9 9.5 %copy-start.2 = (bf16[128,768]{1,0:T(8,128)(2,1)S(1)}, bf16[128,768]{1,0:T(8,128)(2,1)}, u32[]{:S(2)}) copy-start(bf16[128,768]{1,0:T(8,128)(2,1)} %param.9) | copy-start | bytes 589828
  9.9 21.3 %collective-permute-start = (f32[8,4096]{1,0:T(8,128)S(1)}, f32[8,4096]{1,0:T(8,128)S(1)}, u32[]{:S(2)}, u32[]{:S(2)}) collective-permute-start(f32[8,4096]{1,0:T(8,128)S(1)} %mul.67), channel_id=1, source_target_pairs={{0,1},{1,0},{2,3},{3,2},{4,5},{5,4},{6,7},{7,6},{8,9},{9,8},{10,11... | collective-permute-start | bytes 393224 | tf_op jit(solution)/shard_map/ppermute | solution.py:15
  31.2 9.7 %copy-start.3 = (f32[4096]{0:T(1024)S(1)}, f32[4096]{0:T(1024)}, u32[]{:S(2)}) copy-start(f32[4096]{0:T(1024)} %param.6) | copy-start | bytes 49156
  31.2 9.7 %collective-permute-start.1 = (f32[8,4096]{1,0:T(8,128)S(1)}, f32[8,4096]{1,0:T(8,128)S(1)}, u32[]{:S(2)}, u32[]{:S(2)}) collective-permute-start(f32[8,4096]{1,0:T(8,128)S(1)} %add_select_fusion.1), channel_id=1, source_target_pairs={{0,2},{2,0},{1,3},{3,1},{4,6},{6,4},{5,7},{7,5},{8,10},{10,8},{9,1... | collective-permute-start | bytes 393224 | tf_op jit(solution)/shard_map/ppermute | solution.py:15
  44.1 7.4 %collective-permute-start.3 = (bf16[32,8,4096]{2,1,0:T(8,128)(2,1)S(1)}, bf16[32,8,4096]{2,1,0:T(8,128)(2,1)}, u32[]{:S(2)}, u32[]{:S(2)}) collective-permute-start(bf16[32,8,4096]{2,1,0:T(8,128)(2,1)S(1)} %fusion.1), channel_id=1, source_target_pairs={{0,4},{4,0},{1,5},{5,1},{2,6},{6,2},{3,7},{7,3},{8,12},{12,8},{9,1... | collective-permute-start | bytes 6291464 | tf_op jit(solution)/shard_map/ppermute | solution.py:92
  56.3 80.3 %all-to-all-start = ((bf16[32,8,4096]{2,1,0:T(8,128)(2,1)}), bf16[32,8,4096]{2,1,0:T(8,128)(2,1)S(1)}, u32[]{:S(2)}, u32[]{:S(2)}) async-start(bf16[32,8,4096]{2,1,0:T(8,128)(2,1)} %fusion), calls=%async_computation.1 | async-start | bytes 4194304 | tf_op jit(solution)/shard_map/all_to_all | solution.py:93
  67.3 313.1 %all-reduce.2.cloned.1.call-start = ((), (), s32[]{:S(2)}) async-start(), calls=%async_computation.4 | async-start | bytes 131072 | tf_op jit(solution)/shard_map/psum | solution.py:99
  133.8 6.8 %collective-permute-start.2 = (bf16[256,4096]{1,0:T(8,128)(2,1)}, bf16[256,4096]{1,0:T(8,128)(2,1)}, u32[]{:S(2)}, u32[]{:S(2)}) collective-permute-start(bf16[256,4096]{1,0:T(8,128)(2,1)} %all-gather.2.cloned.1.call-done), channel_id=1, source_target_pairs={{0,4},{4,0},{1,5},{5,1},{2,6},{6,2},{3,7},{7,3},{8,12},{12,8},{9,1... | collective-permute-start | bytes 6291464 | tf_op jit(solution)/shard_map/ppermute | solution.py:71
  137.9 37.9 %collective-permute-start.4 = (f32[8,4096]{1,0:T(8,128)S(1)}, f32[8,4096]{1,0:T(8,128)S(1)}, u32[]{:S(2)}, u32[]{:S(2)}) collective-permute-start(f32[8,4096]{1,0:T(8,128)S(1)} %mul.74), channel_id=1, source_target_pairs={{0,1},{1,0},{2,3},{3,2},{4,5},{5,4},{6,7},{7,6},{8,9},{9,8},{10,11... | collective-permute-start | bytes 393224 | tf_op jit(solution)/shard_map/ppermute | solution.py:15
  139.5 0.6 copy-start.1
  140.2 242.3 %reduce-scatter.2.cloned.1.call-start = ((), (), s32[]{:S(2)}) async-start(), calls=%async_computation.3 | async-start | bytes 1966080 | tf_op jit(solution)/shard_map/reduce_scatter | solution.py:77
  144.7 1.9 copy-start
  146.7 6.7 %copy-start.4 = (f32[768]{0:T(1024)S(1)}, f32[768]{0:T(1024)}, u32[]{:S(2)}) copy-start(f32[768]{0:T(1024)} %param.8) | copy-start | bytes 9220
  175.8 206.0 %collective-permute-start.5 = (f32[8,4096]{1,0:T(8,128)S(1)}, f32[8,4096]{1,0:T(8,128)S(1)}, u32[]{:S(2)}, u32[]{:S(2)}) collective-permute-start(f32[8,4096]{1,0:T(8,128)S(1)} %add_select_fusion), channel_id=1, source_target_pairs={{0,2},{2,0},{1,3},{3,1},{4,6},{6,4},{5,7},{7,5},{8,10},{10,8},{9,1... | collective-permute-start | bytes 393224 | tf_op jit(solution)/shard_map/ppermute | solution.py:15
Sparse Core Ops, SparseCore 0:
  47.8 86.0 all-gather.1
  153.5 26.5 reduce-scatter.1
Sparse Core Ops, SparseCore 1:
  140.2 240.1 all-reduce.1
where the time goes:
time: 392 us
  waiting for transfers between devices  275 us (70%)
  matrix products  29.1 us (7%)
  starting transfers between devices  23 us (6%)
  blocking collectives  21.8 us (6%)
  other arithmetic  19.5 us (5%)
  between operations  15.6 us (4%)
  local copies, waits for them, and re-layouts  8.11 us (2%)
    psum x1, waiting for transfers between devices, body(): slots = lax.psum(slots, DP + ('tensor',))  204 us
    all_gather x1, waiting for transfers between devices, body(): half_act = lax.all_gather(quant_act, CHIPS, axis=0, tiled=True)  66.5 us
    dot_general x1, matrix products, body(): lax.dot_general(all_act, all_cot, (((0,), (0,)), ((), ())), preferred_ele...  12.5 us
    all_gather x1, blocking collectives, body(): all_cot = lax.all_gather(cotangent, 'tensor', axis=0, tiled=True)  11.8 us
    all_to_all x1, starting transfers between devices, body(): lax.all_to_all(chip_sum.astype(jnp.bfloat16), CHIPS, 0, 0, tiled=True)  11 us
    psum x1, blocking collectives, body(): clip_weight_grad = lax.psum(weight_terms, 'tensor')  9.99 us
    dot_general x1, matrix products, body(): lax.dot_general(all_cot, quant_weight, (((1,), (1,)), ((), ())), preferre...  8.43 us
  transfers between devices with their start and end apart: 10, of which 4 were waited for; matrix products, arithmetic and copies ran while one was open for 12% of the time, Pallas kernels for 0%

commit v1 on v0

--- a/solution.py
+++ b/solution.py
@@ -96,7 +96,9 @@
     groups = lax.axis_size("tensor")
     slots = jnp.zeros((groups,) + act_terms.shape, act_terms.dtype)
     slots = lax.dynamic_update_index_in_dim(slots, act_terms, lax.axis_index("tensor"), 0)
-    slots = lax.psum(slots, DP + ("tensor",))
+    mesh_axis = DP + ("tensor",)
+    parts = lax.all_gather(slots, mesh_axis, axis=0, tiled=False)
+    slots = parts.sum(axis=0)
     clip_act_grad = lax.dynamic_index_in_dim(slots, lax.axis_index("tensor"), 0, keepdims=False)
     pre_rotation = act_prod * slope_act
     token_grad = rotate(pre_rotation).astype(jnp.bfloat16)

time: 392 us -> 328 us (0.84)
  waiting for transfers between devices: 275 us -> 205 us
  other arithmetic: 19.5 us -> 28.5 us
    psum x1 -> x0, waiting for transfers between devices: 204 us -> none  [body(): slots = lax.psum(slots, DP + ('tensor',))]
    all_gather x0 -> x1, waiting for transfers between devices: none -> 94.3 us  [body(): parts = lax.all_gather(slots, mesh_axis, axis=0, tiled=False)]
    all_to_all x1, waiting for transfers between devices: 0.01 us -> 36.2 us  [body(): lax.all_to_all(chip_sum.astype(jnp.bfloat16), CHIPS, 0, 0, tiled=True)]
    reduce_sum x0 -> x1, other arithmetic: none -> 8.81 us  [body(): slots = parts.sum(axis=0)]
    all_gather x1, waiting for transfers between devices: 66.5 us -> 72 us  [body(): half_act = lax.all_gather(quant_act, CHIPS, axis=0, tiled=True)]
    all_to_all x1, starting transfers between devices: 11 us -> 5.48 us  [body(): lax.all_to_all(chip_sum.astype(jnp.bfloat16), CHIPS, 0, 0, tiled=True)]
  transfers between devices with their start and end apart: 10 -> 10, of which waited for: 4 -> 4; matrix products, arithmetic and copies ran while one was open for 12% -> 15% of each run, Pallas kernels for 0% -> 0%
where the time goes in v1:
time: 328 us; the launch traced here: 327 us
  waiting for transfers between devices  205 us (62%)
  matrix products  29 us (9%)
  other arithmetic  28.5 us (9%)
  starting transfers between devices  22.2 us (7%)
  blocking collectives  19.5 us (6%)
  between operations  15.6 us (5%)
  local copies, waits for them, and re-layouts  7.27 us (2%)
    all_gather x1, waiting for transfers between devices, body(): parts = lax.all_gather(slots, mesh_axis, axis=0, tiled=False)  94.3 us
    all_gather x1, waiting for transfers between devices, body(): half_act = lax.all_gather(quant_act, CHIPS, axis=0, tiled=True)  72 us
    all_to_all x1, waiting for transfers between devices, body(): lax.all_to_all(chip_sum.astype(jnp.bfloat16), CHIPS, 0, 0, tiled=True)  36.2 us
    dot_general x1, matrix products, body(): lax.dot_general(all_act, all_cot, (((0,), (0,)), ((), ())), preferred_ele...  12.4 us
    all_gather x1, blocking collectives, body(): all_cot = lax.all_gather(cotangent, 'tensor', axis=0, tiled=True)  11.8 us
    reduce_sum x1, other arithmetic, body(): slots = parts.sum(axis=0)  8.81 us
    dot_general x1, matrix products, body(): lax.dot_general(all_cot, quant_weight, (((1,), (1,)), ((), ())), preferre...  8.43 us
    ppermute x4, starting transfers between devices, swapped(): return lax.ppermute(block, axis, route)  7.77 us
  transfers between devices with their start and end apart: 10, of which 4 were waited for; matrix products, arithmetic and copies ran while one was open for 15% of the time, Pallas kernels for 0%

profile of v1, /device:TPU:1, one launch (start us, length us, event | category | flops | bytes accessed | tf_op | source)
XLA Modules:
  0.0 327.4 jit_solution(4944738131374757998)
XLA Ops:
  8.0 0.0 all-gather.3.cloned.1.call-start
  8.0 1.0 reshape.43
  9.1 0.3 convolution_bitcast_fusion.1
  9.4 0.4 convolution_multiply_fusion.1
  9.8 0.1 mul.67
  9.9 0.0 copy-start.2
  9.9 2.2 collective-permute-start
  12.1 7.3 %multiply_convert_fusion.1 = bf16[4096,768]{1,0:T(8,128)(2,1)} fusion(f32[768]{0:T(1024)} %param.8, bf16[4096,768]{1,0:T(8,128)(2,1)} %param.7), kind=kLoop, calls=%fused_computation.3 | loop fusion | flops 12582912 | bytes 12585984 | tf_op jit(solution)/shard_map/convert_element_type | solution.py:63
  19.4 0.0 copy-done.2
  19.4 11.8 %all_gather.12 = bf16[512,768]{1,0:T(8,128)(2,1)S(1)} all-gather(bf16[128,768]{1,0:T(8,128)(2,1)S(1)} %copy-done.2), channel_id=1, replica_groups=mesh['dx'=4,'dz'=8,'dc'=2,'tensor'=4] {'tensor'}, dimensions={0}, use_global_device_ids=true | all-gather | bytes 983040 | tf_op jit(solution)/shard_map/all_gather | solution.py:64
  31.2 0.0 collective-permute-done
  31.2 0.0 copy-start.3
  31.2 1.3 collective-permute-start.1
  32.5 8.4 %fusion.35 = f32[4096,512]{0,1:T(8,128)} fusion(bf16[4096,768]{1,0:T(8,128)(2,1)} %multiply_convert_fusion.1, bf16[512,768]{1,0:T(8,128)(2,1)S(1)} %all_gather.12), kind=kOutput, calls=%fused_computation.57 | convolution fusion | flops 3221225472 | bytes 15466496 | tf_op jit(solution)/shard_map/dot_general | solution.py:65
  40.9 0.0 collective-permute-done.1
  40.9 0.0 copy-done.3
  40.9 0.7 multiply_convert_fusion.2
  41.6 0.0 all-gather.3.cloned.1.call-update
  41.7 2.5 fusion.1
  44.1 3.5 %collective-permute-start.3 = (bf16[32,8,4096]{2,1,0:T(8,128)(2,1)S(1)}, bf16[32,8,4096]{2,1,0:T(8,128)(2,1)}, u32[]{:S(2)}, u32[]{:S(2)}) collective-permute-start(bf16[32,8,4096]{2,1,0:T(8,128)(2,1)S(1)} %fusion.1), channel_id=1, source_target_pairs={{0,4},{4,0},{1,5},{5,1},{2,6},{6,2},{3,7},{7,3},{8,12},{12,8},{9,1... | collective-permute-start | bytes 6291464 | tf_op jit(solution)/shard_map/ppermute | solution.py:92
  47.7 72.0 %all-gather.3.cloned.1.call-done = bf16[256,4096]{1,0:T(8,128)(2,1)} async-done(((bf16[8,4096]{1,0:T(8,128)(2,1)}), bf16[256,4096]{1,0:T(8,128)(2,1)}) %all-gather.3.cloned.1.call-update) | async-done | bytes 2097168 | tf_op jit(solution)/shard_map/all_gather | solution.py:69
  119.7 5.3 %collective-permute-start.2 = (bf16[256,4096]{1,0:T(8,128)(2,1)}, bf16[256,4096]{1,0:T(8,128)(2,1)}, u32[]{:S(2)}, u32[]{:S(2)}) collective-permute-start(bf16[256,4096]{1,0:T(8,128)(2,1)} %all-gather.3.cloned.1.call-done), channel_id=1, source_target_pairs={{0,4},{4,0},{1,5},{5,1},{2,6},{6,2},{3,7},{7,3},{8,12},{12,8},{9,1... | collective-permute-start | bytes 6291464 | tf_op jit(solution)/shard_map/ppermute | solution.py:71
  125.0 0.0 collective-permute-done.3
  125.0 4.7 %fusion = bf16[32,8,4096]{2,1,0:T(8,128)(2,1)} fusion(bf16[32,8,4096]{2,1,0:T(8,128)(2,1)} %collective-permute-done.3, f32[32,2,8,4096]{3,2,1,0:T(8,128)} %bitcast.42, s32[]{:T(128)S(6)} %select_n.50), kind=kLoop, calls=%fused_computation.7 | loop fusion | flops 3145728 | bytes 8388612 | tf_op jit(solution)/shard_map/convert_element_type | solution.py:93
  129.7 5.5 %all-to-all-start = ((bf16[32,8,4096]{2,1,0:T(8,128)(2,1)}), bf16[32,8,4096]{2,1,0:T(8,128)(2,1)S(1)}, u32[]{:S(2)}, u32[]{:S(2)}) async-start(bf16[32,8,4096]{2,1,0:T(8,128)(2,1)} %fusion), calls=%async_computation.1 | async-start | bytes 4194304 | tf_op jit(solution)/shard_map/all_to_all | solution.py:93
  135.2 0.0 reduce-scatter.2.cloned.1.call-start
  135.3 0.0 collective-permute-done.2
  135.3 4.2 %maximum_select_fusion = bf16[2,32,8,4096]{3,2,0,1:T(8,128)(2,1)S(1)} fusion(bf16[1,32,8,4096]{3,2,0,1:T(8,128)(2,1)} %bitcast.6, bf16[1,32,8,4096]{3,2,0,1:T(8,128)(2,1)} %bitcast.45, pred[]{:T(512)S(6)} %eq.11), kind=kLoop, calls=%fused_computation.5 | loop fusion | flops 6291456 | bytes 8388609 | tf_op jit(solution)/shard_map/jit(_where)/select_n | solution.py:72
  139.5 0.0 copy-start
  139.5 1.9 copy-done
  141.4 6.6 %fusion.36 = f32[512,768]{1,0:T(8,128)} fusion(bf16[512,4096]{1,0:T(8,128)(2,1)S(1)} %bitcast.43, bf16[4096,768]{1,0:T(8,128)(2,1)} %multiply_convert_fusion.1), kind=kOutput, calls=%fused_computation.58 | convolution fusion | flops 3221225472 | bytes 12058624 | tf_op jit(solution)/shard_map/dot_general | solution.py:78
  148.1 0.0 copy-start.4
  148.1 0.0 reduce-scatter.2.cloned.1.call-update
  148.1 0.0 all-gather.5.cloned.1.call-start
  148.1 36.2 %all-to-all-done = bf16[32,8,4096]{2,1,0:T(8,128)(2,1)S(1)} async-done(((bf16[32,8,4096]{2,1,0:T(8,128)(2,1)}), bf16[32,8,4096]{2,1,0:T(8,128)(2,1)S(1)}, u32[]{:S(2)}, u32[]{:S(2)}) %all-to-all-start) | async-done | bytes 2097184 | tf_op jit(solution)/shard_map/all_to_all | solution.py:93
  184.4 0.3 convert_reduce_fusion
  184.7 0.1 multiply_reduce_fusion.1
  184.8 0.2 dynamic_update_slice.5
  185.0 0.0 copy-start.1
  185.0 0.6 copy-done.1
  185.7 0.0 all-gather.5.cloned.1.call-update
  185.7 0.1 reshape.46
  185.8 0.4 convolution_bitcast_fusion
  186.2 0.4 convolution_multiply_fusion
  186.6 0.1 mul.74
  186.7 1.3 collective-permute-start.4
  188.0 2.6 collective-permute-done.4
  190.6 3.0 collective-permute-start.5
  193.7 0.0 copy-done.4
  193.7 12.4 %multiply_reduce_fusion = (f32[768]{0:T(1024)S(1)}, bf16[4096,768]{1,0:T(8,128)(2,1)}) fusion(f32[768]{0:T(1024)S(1)} %copy-done.4, bf16[4096,768]{1,0:T(8,128)(2,1)} %param.7, bf16[512,4096]{1,0:T(8,128)(2,1)} %bitcast.44, bf16[512,768]{1,0:T(8,128)(2,1)S(1)} %all_gather.12), kind=kOutput, calls=%fused_computation | convolution fusion | flops 3252681984 | bytes 17569792 | tf_op jit(solution)/shard_map/dot_general | solution.py:83
  206.1 7.7 %psum.7 = f32[768]{0:T(1024)} all-reduce(f32[768]{0:T(1024)S(1)} %get-tuple-element.11), channel_id=1, replica_groups=mesh['dx'=4,'dz'=8,'dc'=2,'tensor'=4] {'tensor'}, use_global_device_ids=true, to_apply=%region_5.6 | all-reduce | flops 768 | bytes 6144 | tf_op jit(solution)/shard_map/psum | solution.py:89
  213.8 0.0 collective-permute-done.5
  213.8 0.6 select_convert_fusion
  214.5 0.0 reduce-scatter.2.cloned.1.call-done
  214.5 1.7 convert_element_type.50
  216.2 94.3 %all-gather.5.cloned.1.call-done = f32[256,4,4096]{2,1,0:T(4,128)} async-done(((f32[1,4,4096]{2,1,0:T(4,128)}), f32[256,4,4096]{2,1,0:T(4,128)}) %all-gather.5.cloned.1.call-update) | async-done | bytes 16777232 | tf_op jit(solution)/shard_map/all_gather | solution.py:100
  310.5 8.8 %reduce_sum.38 = f32[4,4096]{1,0:T(4,128)S(1)} reduce(f32[256,4,4096]{2,1,0:T(4,128)} %all-gather.5.cloned.1.call-done, f32[]{:T(128)} %constant.45.clone.1), dimensions={0}, to_apply=%region_3.4 | reduce | flops 4177920 | bytes 16842756 | tf_op jit(solution)/shard_map/reduce_sum | solution.py:101
  319.3 0.6 constant_dynamic-slice_fusion
  (3 shorter events, 0.0 us)
Async XLA Ops:
  8.0 111.7 %all-gather.3.cloned.1.call-start = ((), (), s32[]{:S(2)}) async-start(), calls=%async_computation.2 | async-start | bytes 2162688 | tf_op jit(solution)/shard_map/all_gather | solution.py:69
  9.9 9.5 %copy-start.2 = (bf16[128,768]{1,0:T(8,128)(2,1)S(1)}, bf16[128,768]{1,0:T(8,128)(2,1)}, u32[]{:S(2)}) copy-start(bf16[128,768]{1,0:T(8,128)(2,1)} %param.9) | copy-start | bytes 589828
  9.9 21.3 %collective-permute-start = (f32[8,4096]{1,0:T(8,128)S(1)}, f32[8,4096]{1,0:T(8,128)S(1)}, u32[]{:S(2)}, u32[]{:S(2)}) collective-permute-start(f32[8,4096]{1,0:T(8,128)S(1)} %mul.67), channel_id=1, source_target_pairs={{0,1},{1,0},{2,3},{3,2},{4,5},{5,4},{6,7},{7,6},{8,9},{9,8},{10,11... | collective-permute-start | bytes 393224 | tf_op jit(solution)/shard_map/ppermute | solution.py:15
  31.2 9.7 %copy-start.3 = (f32[4096]{0:T(1024)S(1)}, f32[4096]{0:T(1024)}, u32[]{:S(2)}) copy-start(f32[4096]{0:T(1024)} %param.6) | copy-start | bytes 49156
  31.2 9.7 %collective-permute-start.1 = (f32[8,4096]{1,0:T(8,128)S(1)}, f32[8,4096]{1,0:T(8,128)S(1)}, u32[]{:S(2)}, u32[]{:S(2)}) collective-permute-start(f32[8,4096]{1,0:T(8,128)S(1)} %add_select_fusion.1), channel_id=1, source_target_pairs={{0,2},{2,0},{1,3},{3,1},{4,6},{6,4},{5,7},{7,5},{8,10},{10,8},{9,1... | collective-permute-start | bytes 393224 | tf_op jit(solution)/shard_map/ppermute | solution.py:15
  44.1 80.9 %collective-permute-start.3 = (bf16[32,8,4096]{2,1,0:T(8,128)(2,1)S(1)}, bf16[32,8,4096]{2,1,0:T(8,128)(2,1)}, u32[]{:S(2)}, u32[]{:S(2)}) collective-permute-start(bf16[32,8,4096]{2,1,0:T(8,128)(2,1)S(1)} %fusion.1), channel_id=1, source_target_pairs={{0,4},{4,0},{1,5},{5,1},{2,6},{6,2},{3,7},{7,3},{8,12},{12,8},{9,1... | collective-permute-start | bytes 6291464 | tf_op jit(solution)/shard_map/ppermute | solution.py:92
  119.7 15.6 %collective-permute-start.2 = (bf16[256,4096]{1,0:T(8,128)(2,1)}, bf16[256,4096]{1,0:T(8,128)(2,1)}, u32[]{:S(2)}, u32[]{:S(2)}) collective-permute-start(bf16[256,4096]{1,0:T(8,128)(2,1)} %all-gather.3.cloned.1.call-done), channel_id=1, source_target_pairs={{0,4},{4,0},{1,5},{5,1},{2,6},{6,2},{3,7},{7,3},{8,12},{12,8},{9,1... | collective-permute-start | bytes 6291464 | tf_op jit(solution)/shard_map/ppermute | solution.py:71
  129.7 54.6 %all-to-all-start = ((bf16[32,8,4096]{2,1,0:T(8,128)(2,1)}), bf16[32,8,4096]{2,1,0:T(8,128)(2,1)S(1)}, u32[]{:S(2)}, u32[]{:S(2)}) async-start(bf16[32,8,4096]{2,1,0:T(8,128)(2,1)} %fusion), calls=%async_computation.1 | async-start | bytes 4194304 | tf_op jit(solution)/shard_map/all_to_all | solution.py:93
  135.2 79.3 %reduce-scatter.2.cloned.1.call-start = ((), (), s32[]{:S(2)}) async-start(), calls=%async_computation.3 | async-start | bytes 1966080 | tf_op jit(solution)/shard_map/reduce_scatter | solution.py:77
  139.5 1.9 copy-start
  148.1 45.6 %copy-start.4 = (f32[768]{0:T(1024)S(1)}, f32[768]{0:T(1024)}, u32[]{:S(2)}) copy-start(f32[768]{0:T(1024)} %param.8) | copy-start | bytes 9220
  148.1 162.4 %all-gather.5.cloned.1.call-start = ((), (), s32[]{:S(2)}) async-start(), calls=%async_computation.4 | async-start | bytes 16842752 | tf_op jit(solution)/shard_map/all_gather | solution.py:100
  185.0 0.6 copy-start.1
  186.7 3.9 %collective-permute-start.4 = (f32[8,4096]{1,0:T(8,128)S(1)}, f32[8,4096]{1,0:T(8,128)S(1)}, u32[]{:S(2)}, u32[]{:S(2)}) collective-permute-start(f32[8,4096]{1,0:T(8,128)S(1)} %mul.74), channel_id=1, source_target_pairs={{0,1},{1,0},{2,3},{3,2},{4,5},{5,4},{6,7},{7,6},{8,9},{9,8},{10,11... | collective-permute-start | bytes 393224 | tf_op jit(solution)/shard_map/ppermute | solution.py:15
  190.6 23.2 %collective-permute-start.5 = (f32[8,4096]{1,0:T(8,128)S(1)}, f32[8,4096]{1,0:T(8,128)S(1)}, u32[]{:S(2)}, u32[]{:S(2)}) collective-permute-start(f32[8,4096]{1,0:T(8,128)S(1)} %add_select_fusion), channel_id=1, source_target_pairs={{0,2},{2,0},{1,3},{3,1},{4,6},{6,4},{5,7},{7,5},{8,10},{10,8},{9,1... | collective-permute-start | bytes 393224 | tf_op jit(solution)/shard_map/ppermute | solution.py:15
Sparse Core Ops, SparseCore 0:
  41.8 77.8 all-gather.2
  148.2 28.2 reduce-scatter.1
Sparse Core Ops, SparseCore 1:
  185.8 124.7 all-gather.4
